TPU v7x, 128 devices: a whole 4x4x4 slice. The times are simulated.
128 devices in a mesh: row: 8 (over z, core), col: 16 (over x, y).
Axes of the slice: x: 4, y: 4, z: 4, core: 2. Of those that a mesh axis runs over, the one named last changes fastest.
Arguments:
- tokens: bfloat16 [4096, 2048], P('col', 'row'), may hold values from -6 to 6
- router: bfloat16 [2048, 32], replicated, may hold values from -0.125 to 0.125
- shared_gate_vector: bfloat16 [2048], replicated, may hold values from -0.125 to 0.125
- shared_gate_weight: bfloat16 [2048, 5632], P('col', 'row'), may hold values from -0.125 to 0.125
- shared_up_weight: bfloat16 [2048, 5632], P('col', 'row'), may hold values from -0.125 to 0.125
- shared_down_weight: bfloat16 [5632, 2048], P('row', 'col'), may hold values from -0.078125 to 0.078125
- routed_gate_weight: bfloat16 [32, 2048, 1408], P('col', None, 'row'), may hold values from -0.125 to 0.125
- routed_up_weight: bfloat16 [32, 2048, 1408], P('col', None, 'row'), may hold values from -0.125 to 0.125
- routed_down_weight: bfloat16 [32, 1408, 2048], P('col', 'row'), may hold values from -0.15625 to 0.15625
- adapter_input_factor: bfloat16 [64, 16, 2048], P(None, None, 'row'), may hold values from -0.125 to 0.125
- adapter_output_factor: bfloat16 [64, 16, 5632], P(None, None, 'row'), may hold values from -0.29882812 to 0.29882812
- routes: int32 [4096, 4], P('col'), may hold values from 0 to 31, all different within a row; in each aligned block of 256 rows (0 to 255, 256 to 511, ...) at most 64 rows name the same one
- lengths: int32 [16, 16], P('col'), may hold values from 1 to 128, 256 in all within a row
- prompt_adapter_index: int32 [16, 16], P('col'), may hold values from 0 to 15
- active_adapter_index: int32 [16], replicated, may hold values from 0 to 63, as said below
Outputs:
- moe_out: float32 [4096, 2048], P('col', 'row')
Inputs may be any that keep to these rules, and one draw needn't show every extreme that they name: `routes`: in each group of 256 consecutive tokens no expert is named by more than 64 tokens, a bound that some block reaches. Each group's 16 lengths sum to 256; the longest is exactly 128. `active_adapter_index`: the 16 entries are distinct.
All inputs are finite; a program needn't handle non-finite values.
Results may differ from a plain program's by a relative error of at most 0.003.
Values may be sent and summed in bfloat16 or wider, within the bound.
No kernel may reach another device: no remote copies, remote signals or barrier semaphores. Data moves between devices by JAX's collectives and lax.ppermute only.
A program may use at most 128 MiB of HBM per device.

v0:
```python
import jax
import jax.numpy as jnp
from jax import lax
from jax.sharding import PartitionSpec as P

ADAPTER_SCALE = 2.0


def on_device(
    tokens,
    router,
    shared_gate_vector,
    shared_gate_weight,
    shared_up_weight,
    shared_down_weight,
    routed_gate_weight,
    routed_up_weight,
    routed_down_weight,
    adapter_input_factor,
    adapter_output_factor,
    routes,
    lengths,
    prompt_adapter_index,
    active_adapter_index,
):
    all_features = lax.all_gather(tokens, "row", axis=1, tiled=True)
    token_count = all_features.shape[0]
    full_width = all_features.shape[1]
    local_width = tokens.shape[1]
    col_count = lax.axis_size("col")
    local_experts = routed_gate_weight.shape[0]
    expert_count = local_experts * col_count
    route_count = routes.shape[1]
    capacity = 2 * token_count * route_count // expert_count
    logits = jnp.dot(all_features, router, preferred_element_type=jnp.float32)
    onehot = routes[:, :, None] == jnp.arange(expert_count, dtype=jnp.int32)[None, None, :]
    picked = jnp.sum(jnp.where(onehot, logits[:, None, :], 0.0), axis=2)
    raw_exp = jnp.exp(picked)
    gate_weights = raw_exp / jnp.sum(raw_exp, axis=1, keepdims=True)
    share = jax.nn.sigmoid(
        jnp.dot(all_features, shared_gate_vector, preferred_element_type=jnp.float32)
    )
    hit_table = jnp.any(onehot, axis=1).astype(jnp.int32)
    running_count = jnp.cumsum(hit_table, axis=0)
    slot_rank = running_count - hit_table
    route_rank = jnp.sum(jnp.where(onehot, slot_rank[:, None, :], 0), axis=2)
    row_index = routes * capacity + route_rank
    request_ends = jnp.cumsum(lengths[0])
    request_count = lengths.shape[1]
    token_position = jnp.arange(token_count, dtype=jnp.int32)
    request_of = jnp.sum(
        (token_position[:, None] >= request_ends[None, :]).astype(jnp.int32), axis=1
    )
    request_match = request_of[:, None] == jnp.arange(request_count, dtype=jnp.int32)[None, :]
    adapter_of = jnp.sum(jnp.where(request_match, prompt_adapter_index[0][None, :], 0), axis=1)
    picked_input_factor = jnp.take(adapter_input_factor, active_adapter_index, axis=0)
    rank_width = picked_input_factor.shape[1]
    reduced_rank_value = picked_input_factor.shape[0] * rank_width
    full_in = lax.all_gather(picked_input_factor, "row", axis=2, tiled=True).reshape(
        reduced_rank_value, full_width
    )
    low_rank = lax.dot_general(
        all_features, full_in, (((1,), (1,)), ((), ())), preferred_element_type=jnp.float32
    )
    owner = jnp.arange(reduced_rank_value, dtype=jnp.int32) // rank_width
    adapter_mask = adapter_of[:, None] == owner[None, :]
    low_masked = jnp.where(adapter_mask, low_rank.astype(jnp.bfloat16), jnp.zeros((), jnp.bfloat16))
    picked_output_factor = jnp.take(adapter_output_factor, active_adapter_index, axis=0).reshape(
        reduced_rank_value, adapter_output_factor.shape[2]
    )
    adapter_update = jnp.dot(low_masked, picked_output_factor, preferred_element_type=jnp.float32)
    shared_gate_value = jnp.dot(
        all_features,
        lax.all_gather(shared_gate_weight, "col", axis=0, tiled=True),
        preferred_element_type=jnp.float32,
    )
    shared_up_value = jnp.dot(
        all_features,
        lax.all_gather(shared_up_weight, "col", axis=0, tiled=True),
        preferred_element_type=jnp.float32,
    )
    shared_hidden_units = (
        jax.nn.silu(shared_gate_value) * (shared_up_value + ADAPTER_SCALE * adapter_update)
    ).astype(jnp.bfloat16)
    shared_part = jnp.dot(
        shared_hidden_units,
        lax.all_gather(shared_down_weight, "col", axis=1, tiled=True),
        preferred_element_type=jnp.float32,
    )
    shared_part = shared_part * share[:, None]
    positions = jnp.arange(capacity, dtype=jnp.int32)
    slot_token = jnp.sum(
        (running_count.T[:, None, :] <= positions[None, :, None]).astype(jnp.int32), axis=2
    )
    slot_valid = positions[None, :] < running_count[-1][:, None]
    picked_rows = jnp.take(all_features, jnp.minimum(slot_token, token_count - 1), axis=0)
    chosen = jnp.where(slot_valid[:, :, None], picked_rows, jnp.zeros((), jnp.bfloat16))
    outgoing = chosen.reshape(col_count, local_experts, capacity, full_width)
    slot_block = lax.all_to_all(outgoing, "col", split_axis=0, concat_axis=0, tiled=True)
    gate_part = jnp.einsum(
        "sexd,edf->sexf", slot_block, routed_gate_weight, preferred_element_type=jnp.float32
    )
    up_part = jnp.einsum(
        "sexd,edf->sexf", slot_block, routed_up_weight, preferred_element_type=jnp.float32
    )
    hidden = (jax.nn.silu(gate_part) * up_part).astype(jnp.bfloat16)
    partial_value = jnp.einsum(
        "sexf,efd->sexd", hidden, routed_down_weight, preferred_element_type=jnp.float32
    )
    summed, shared_sum = (
        lax.psum_scatter(partial_value, "row", scatter_dimension=3, tiled=True),
        lax.psum_scatter(shared_part, "row", scatter_dimension=1, tiled=True),
    )
    returned = lax.all_to_all(summed, "col", split_axis=0, concat_axis=0, tiled=True)
    flat_rows = returned.reshape(expert_count * capacity, local_width)
    routed_rows = jnp.take(flat_rows, row_index, axis=0)
    routed = jnp.sum(gate_weights[:, :, None] * routed_rows, axis=1)
    return routed + shared_sum


def solution(mesh):
    return jax.shard_map(
        on_device,
        mesh=mesh,
        in_specs=(
            P("col", "row"),
            P(),
            P(),
            P("col", "row"),
            P("col", "row"),
            P("row", "col"),
            P("col", None, "row"),
            P("col", None, "row"),
            P("col", "row", None),
            P(None, None, "row"),
            P(None, None, "row"),
            P("col", None),
            P("col", None),
            P("col", None),
            P(),
        ),
        out_specs=P("col", "row"),
        check_vma=False,
    )
```

profile of v0, /device:TPU:0, one launch (start us, length us, event | category | flops | bytes accessed | tf_op | source)
XLA Modules:
  0.0 487.8 jit_solution(12929686134690936716)
XLA Ops:
  6.5 0.7 all-gather.6.cloned.1.call-update
  7.3 0.7 compare_select_fusion.3
  8.0 1.6 gather_fusion.2
  9.6 0.7 compare_and_fusion.2
  10.2 0.7 broadcast_select_fusion
  11.1 0.7 all-gather.8.cloned.1.call-update
  12.3 0.7 fusion.29
  13.1 0.6 reduce-window.18
  14.0 0.6 convert_reduce_fusion
  15.1 20.0 %all-gather.6.cloned.1.call-done = bf16[256,2048]{1,0:T(8,128)(2,1)} async-done(((bf16[256,256]{1,0:T(8,128)(2,1)}), bf16[256,2048]{1,0:T(8,128)(2,1)}) %all-gather.6.cloned.1.call-update) | async-done | bytes 1048592 | tf_op jit(solution)/shard_map/all_gather | solution.py:26
  35.0 17.7 %gather_fusion = bf16[2048,2048]{1,0:T(8,128)(2,1)} fusion(bf16[256,2048]{1,0:T(8,128)(2,1)} %all-gather.6.cloned.1.call-done, s32[2048]{0:T(1024)S(1)} %broadcast_clamp_fusion), kind=kCustom, calls=%fused_computation | custom fusion | bytes 16785408 | tf_op jit(solution)/shard_map/jit(_take)/gather | solution.py:96
  52.7 7.5 %select_select_fusion = bf16[16,2,64,2048]{3,2,1,0:T(8,128)(2,1)} fusion(bf16[16,2,64,2048]{3,2,1,0:T(8,128)(2,1)} %bitcast.88, pred[16,2,64]{2,1,0:T(4,128)(4,1)S(1)} %get-tuple-element.9, pred[16,2,64]{2,1,0:T(4,128)(4,1)S(1)} %get-tuple-element.10), kind=kLoop, calls=%fused_computation.4 | loop fusion | flops 8388608 | bytes 16781312 | tf_op jit(solution)/shard_map/jit(_where)/select_n | solution.py:97
  60.2 7.0 %all-to-all-start = ((bf16[16,2,64,2048]{3,2,1,0:T(8,128)(2,1)}), bf16[16,2,64,2048]{3,2,1,0:T(8,128)(2,1)}, u32[]{:S(2)}, u32[]{:S(2)}) async-start(bf16[16,2,64,2048]{3,2,1,0:T(8,128)(2,1)} %select_select_fusion), calls=%async_computation | async-start | bytes 16777216 | tf_op jit(solution)/shard_map/all_to_all | solution.py:99
  67.3 0.5 all-gather.14.cloned.1.call-update
  67.9 152.1 %all-to-all-done = bf16[16,2,64,2048]{3,2,1,0:T(8,128)(2,1)} async-done(((bf16[16,2,64,2048]{3,2,1,0:T(8,128)(2,1)}), bf16[16,2,64,2048]{3,2,1,0:T(8,128)(2,1)}, u32[]{:S(2)}, u32[]{:S(2)}) %all-to-all-start) | async-done | bytes 8388640 | tf_op jit(solution)/shard_map/all_to_all | solution.py:99
  219.9 7.0 %fusion.2 = f32[2,16,64,176]{3,2,1,0:T(8,128)} fusion(bf16[16,2,64,2048]{3,2,1,0:T(8,128)(2,1)} %all-to-all-done, bf16[2,2048,176]{1,2,0:T(8,128)(2,1)S(1)} %copy-done.7), kind=kOutput, calls=%fused_computation.7 | convolution fusion | flops 1476395008 | bytes 11272192 | tf_op jit(solution)/shard_map/sexd,edf->sexf/dot_general | solution.py:100
  227.0 15.2 %convolution_bitcast_fusion = f32[16,2,64,2048]{3,2,0,1:T(8,128)} fusion(f32[2,16,64,176]{3,2,1,0:T(8,128)} %fusion.2, bf16[16,2,64,2048]{3,2,1,0:T(8,128)(2,1)} %all-to-all-done, bf16[2,176,2048]{2,1,0:T(8,128)(2,1)} %param.23, bf16[2,2048,176]{1,2,0:T(8,128)(2,1)} %param.22), kind=kOutput, calls=%fused_computation.9 | convolution fusion | flops 2954952704 | bytes 29491200 | tf_op jit(solution)/shard_map/sexf,efd->sexd/dot_general | solution.py:107
  243.1 0.6 gather_fusion.3
  244.4 1.7 fusion.20
  246.2 3.6 fusion.35
  249.8 35.6 %all-gather.10.cloned.1.call-done = bf16[2048,704]{0,1:T(8,128)(2,1)} async-done(((bf16[128,704]{0,1:T(8,128)(2,1)}), bf16[2048,704]{0,1:T(8,128)(2,1)}) %all-gather.10.cloned.1.call-update) | async-done | bytes 2883600 | tf_op jit(solution)/shard_map/all_gather | solution.py:79
  285.5 3.6 fusion.36
  289.1 48.2 %all-gather.14.cloned.1.call-done = bf16[704,2048]{1,0:T(8,128)(2,1)} async-done(((bf16[704,128]{1,0:T(8,128)(2,1)}), bf16[704,2048]{1,0:T(8,128)(2,1)}) %all-gather.14.cloned.1.call-update) | async-done | bytes 2883600 | tf_op jit(solution)/shard_map/all_gather | solution.py:87
  337.3 4.9 %convolution_multiply_fusion = f32[256,2048]{1,0:T(8,128)} fusion(bf16[704,2048]{1,0:T(8,128)(2,1)} %all-gather.14.cloned.1.call-done, f32[256,704]{0,1:T(8,128)} %fusion.36, bf16[256,256]{0,1:T(8,128)(2,1)S(1)} %fusion.20, bf16[256,704]{1,0:T(8,128)(2,1)S(1)} %bitcast_select_fusion, f32[256]{0:T(256)S(1)} %add_divide_fusion, f32[256,704]{0,1:T(8,128)} %fusion.35), kind=kOutput, calls=%fused_computation.10 | convolution fusion | flops 832438272 | bytes 6915072 | tf_op jit(solution)/shard_map/dot_general | solution.py:85
  342.2 88.8 %reduce-scatter.3.cloned.1.call-done = f32[16,2,64,256]{3,2,0,1:T(8,128)} async-done(((f32[16,2,64,2048]{3,2,0,1:T(8,128)}), f32[16,2,64,256]{3,2,0,1:T(8,128)}) %reduce-scatter.3.cloned.1.call-update) | async-done | bytes 2097168 | tf_op jit(solution)/shard_map/reduce_scatter | solution.py:111
  431.0 3.2 copy.52
  434.2 7.0 %all-to-all-start.1 = ((f32[16,2,64,256]{3,2,1,0:T(8,128)}), f32[16,2,64,256]{3,2,1,0:T(8,128)}, u32[]{:S(2)}, u32[]{:S(2)}) async-start(f32[16,2,64,256]{3,2,1,0:T(8,128)} %copy.52), calls=%async_computation.2 | async-start | bytes 4194304 | tf_op jit(solution)/shard_map/all_to_all | solution.py:114
  442.5 27.9 %all-to-all-done.1 = f32[16,2,64,256]{3,2,1,0:T(8,128)} async-done(((f32[16,2,64,256]{3,2,1,0:T(8,128)}), f32[16,2,64,256]{3,2,1,0:T(8,128)}, u32[]{:S(2)}, u32[]{:S(2)}) %all-to-all-start.1) | async-done | bytes 2097184 | tf_op jit(solution)/shard_map/all_to_all | solution.py:114
  470.3 5.1 %gather_fusion.1 = f32[1024,256]{1,0:T(8,128)S(1)} fusion(f32[2048,256]{1,0:T(8,128)} %bitcast.14, s32[1024]{0:T(1024)S(1)} %broadcast_clamp_fusion.1), kind=kCustom, calls=%fused_computation.1 | custom fusion | bytes 2101248 | tf_op jit(solution)/shard_map/jit(_take)/gather | solution.py:116
  475.4 1.3 reshape.164
  476.7 2.5 multiply_reduce_fusion
  479.2 1.7 add.77
  (67 shorter events, 4.4 us)
Async XLA Ops:
  6.5 236.6 %copy-start = (bf16[64,16,704]{2,1,0:T(8,128)(2,1)S(1)}, bf16[64,16,704]{2,1,0:T(8,128)(2,1)}, u32[]{:S(2)}) copy-start(bf16[64,16,704]{2,1,0:T(8,128)(2,1)} %param.25) | copy-start | bytes 4325380
  6.5 28.5 %all-gather.6.cloned.1.call-start = ((), (), s32[]{:S(2)}) async-start(), calls=%async_computation.4 | async-start | bytes 1179648 | tf_op jit(solution)/shard_map/all_gather | solution.py:26
  7.3 237.2 %all-gather.12.cloned.1.call-start = ((), (), s32[]{:S(2)}) async-start(), calls=%async_computation.8 | async-start | bytes 1179648 | tf_op jit(solution)/shard_map/all_gather | solution.py:59
  11.0 235.2 %all-gather.8.cloned.1.call-start = ((), (), s32[]{:S(2)}) async-start(), calls=%async_computation.6 | async-start | bytes 3063808 | tf_op jit(solution)/shard_map/all_gather | solution.py:74
  11.8 273.7 %all-gather.10.cloned.1.call-start = ((), (), s32[]{:S(2)}) async-start(), calls=%async_computation.7 | async-start | bytes 3063808 | tf_op jit(solution)/shard_map/all_gather | solution.py:79
  60.2 159.7 %copy-start.7 = (bf16[2,2048,176]{1,2,0:T(8,128)(2,1)S(1)}, bf16[2,2048,176]{1,2,0:T(8,128)(2,1)}, u32[]{:S(2)}) copy-start(bf16[2,2048,176]{1,2,0:T(8,128)(2,1)} %param.21) | copy-start | bytes 4325380
  60.2 159.7 %all-to-all-start = ((bf16[16,2,64,2048]{3,2,1,0:T(8,128)(2,1)}), bf16[16,2,64,2048]{3,2,1,0:T(8,128)(2,1)}, u32[]{:S(2)}, u32[]{:S(2)}) async-start(bf16[16,2,64,2048]{3,2,1,0:T(8,128)(2,1)} %select_select_fusion), calls=%async_computation | async-start | bytes 16777216 | tf_op jit(solution)/shard_map/all_to_all | solution.py:99
  67.2 270.1 %all-gather.14.cloned.1.call-start = ((), (), s32[]{:S(2)}) async-start(), calls=%async_computation.9 | async-start | bytes 3063808 | tf_op jit(solution)/shard_map/all_gather | solution.py:87
  67.8 363.2 %reduce-scatter.3.cloned.1.call-start = ((), (), s32[]{:S(2)}) async-start(), calls=%async_computation.5 | async-start | bytes 18874368 | tf_op jit(solution)/shard_map/reduce_scatter | solution.py:111
  242.2 0.7 copy-start.4
  242.2 0.7 copy-start.5
  242.2 1.6 copy-start.6
  242.2 1.8 copy-start.1
  242.2 237.0 %reduce-scatter.5.cloned.1.call-start = ((), (), s32[]{:S(2)}) async-start(), calls=%async_computation.10 | async-start | bytes 2359296 | tf_op jit(solution)/shard_map/reduce_scatter | solution.py:112
  434.2 7.1 %copy-start.3 = (s32[256,4]{0,1:T(4,128)S(1)}, s32[256,4]{0,1:T(4,128)}, u32[]{:S(2)}) copy-start(s32[256,4]{0,1:T(4,128)} %param.26) | copy-start | bytes 12292
  434.2 7.6 %copy-start.2 = (bf16[2048,32]{0,1:T(8,128)(2,1)S(1)}, bf16[2048,32]{0,1:T(8,128)(2,1)}, u32[]{:S(2)}) copy-start(bf16[2048,32]{0,1:T(8,128)(2,1)} %param.16) | copy-start | bytes 393220
  434.2 36.1 %all-to-all-start.1 = ((f32[16,2,64,256]{3,2,1,0:T(8,128)}), f32[16,2,64,256]{3,2,1,0:T(8,128)}, u32[]{:S(2)}, u32[]{:S(2)}) async-start(f32[16,2,64,256]{3,2,1,0:T(8,128)} %copy.52), calls=%async_computation.2 | async-start | bytes 4194304 | tf_op jit(solution)/shard_map/all_to_all | solution.py:114
Sparse Core Ops, SparseCore 0:
  9.0 25.9 all-gather.5
  36.7 24.2 all-gather.11
  63.1 155.2 all-gather.7
  220.5 64.9 all-gather.9
  287.4 49.8 all-gather.13
  339.6 91.3 reduce-scatter.2
  433.4 34.4 reduce-scatter.4
where the time goes:
time: 488 us
  waiting for transfers between devices  375 us (77%)
  matrix products  36.9 us (8%)
  local copies, waits for them, and re-layouts  31 us (6%)
  other arithmetic  16.6 us (3%)
  starting transfers between devices  14.4 us (3%)
  between operations  13.7 us (3%)
    all_to_all x1, waiting for transfers between devices, on_device(): lax.all_to_all(outgoing, 'col', split_axis=0, concat_axis=0, tiled=True)  152 us
    reduce_scatter x1, waiting for transfers between devices, on_device(): lax.psum_scatter(partial_value, 'row', scatter_dimension=3, tiled=True)  88.8 us
    all_gather x1, waiting for transfers between devices, on_device(): lax.all_gather(shared_down_weight, 'col', axis=1, tiled=True)  48.2 us
    all_gather x1, waiting for transfers between devices, on_device(): lax.all_gather(shared_up_weight, 'col', axis=0, tiled=True)  35.6 us
    all_to_all x1, waiting for transfers between devices, on_device(): lax.all_to_all(summed, 'col', split_axis=0, concat_axis=0, tiled=True)  27.9 us
    all_gather x1, waiting for transfers between devices, on_device(): all_features = lax.all_gather(tokens, 'row', axis=1, tiled=True)  20 us
    gather x1, local copies, waits for them, and re-layouts, on_device(): jnp.take(all_features, jnp.minimum(slot_token, token_count - 1), axis=0)  17.7 us
    dot_general x1, matrix products, on_device(): jnp.einsum('sexf,efd->sexd', hidden, routed_down_weight, preferred_elemen...  15.2 us
  transfers between devices with their start and end apart: 9, of which 6 were waited for; matrix products, arithmetic and copies ran while one was open for 17% of the time, Pallas kernels for 0%

commit v1 on v0

--- a/solution.py
+++ b/solution.py
@@ -4,6 +4,12 @@
 from jax.sharding import PartitionSpec as P
 
 ADAPTER_SCALE = 2.0
+
+
+def in_order(blocks, dim):
+    shape = list(blocks.shape[1:])
+    shape[dim] *= blocks.shape[0]
+    return jnp.moveaxis(blocks, 0, dim).reshape(shape)
 
 
 def on_device(
@@ -23,7 +29,19 @@
     prompt_adapter_index,
     active_adapter_index,
 ):
-    all_features = lax.all_gather(tokens, "row", axis=1, tiled=True)
+    devices = lax.axis_size("row")
+    pairs = [(i, (i + 1) % devices) for i in range(devices)]
+    back = [(b, a) for a, b in pairs]
+    lower, upper = ([], [])
+    for step in range(devices - 1):
+        if step % 2 == 0:
+            lower.append(lax.ppermute(lower[-1] if lower else tokens, "row", pairs))
+        else:
+            upper.append(lax.ppermute(upper[-1] if upper else tokens, "row", back))
+    pieces = jnp.stack([*lower[::-1], tokens, *upper])
+    shift = lax.axis_index("row") - len(lower)
+    pieces = pieces[(jnp.arange(devices) - shift) % devices]
+    all_features = in_order(pieces, 1)
     token_count = all_features.shape[0]
     full_width = all_features.shape[1]
     local_width = tokens.shape[1]

time: 488 us -> 462 us (0.947)
  waiting for transfers between devices: 375 us -> 342 us
  starting transfers between devices: 14.4 us -> 23.9 us
    all_gather x1, waiting for transfers between devices: 0.02 us -> 38 us  [on_device(): lax.all_gather(shared_gate_weight, 'col', axis=0, tiled=True)]
    all_gather x1, waiting for transfers between devices: 35.6 us -> 0.02 us  [on_device(): lax.all_gather(shared_up_weight, 'col', axis=0, tiled=True)]
    all_to_all x1, waiting for transfers between devices: 152 us -> 126 us  [on_device(): lax.all_to_all(outgoing, 'col', split_axis=0, concat_axis=0, tiled=True)]
    all_gather x1 -> x0, waiting for transfers between devices: 20 us -> none  [on_device(): all_features = lax.all_gather(tokens, 'row', axis=1, tiled=True)]
    ppermute x0 -> x7, waiting for transfers between devices: none -> 12 us  [the longest x4 12 us: on_device(): lower.append(lax.ppermute(lower[-1] if lower else tokens, 'row', pairs))]
    ppermute x0 -> x7, starting transfers between devices: none -> 9.55 us  [the longest x3 9.52 us: on_device(): upper.append(lax.ppermute(upper[-1] if upper else tokens, 'row', back))]
    gather x1, local copies, waits for them, and re-layouts: 17.7 us -> 11 us  [on_device(): jnp.take(all_features, jnp.minimum(slot_token, token_count - 1), axis=0)]
  transfers between devices with their start and end apart: 9 -> 15, of which waited for: 6 -> 9; matrix products, arithmetic and copies ran while one was open for 17% -> 16% of each run, Pallas kernels for 0% -> 0%
where the time goes in v1:
time: 462 us; the launch traced here: 461 us
  waiting for transfers between devices  342 us (74%)
  matrix products  37.5 us (8%)
  local copies, waits for them, and re-layouts  27.4 us (6%)
  starting transfers between devices  23.9 us (5%)
  other arithmetic  16.7 us (4%)
  between operations  13.8 us (3%)
    all_to_all x1, waiting for transfers between devices, on_device(): lax.all_to_all(outgoing, 'col', split_axis=0, concat_axis=0, tiled=True)  126 us
    reduce_scatter x1, waiting for transfers between devices, on_device(): lax.psum_scatter(partial_value, 'row', scatter_dimension=3, tiled=True)  88.8 us
    all_gather x1, waiting for transfers between devices, on_device(): lax.all_gather(shared_down_weight, 'col', axis=1, tiled=True)  48.2 us
    all_gather x1, waiting for transfers between devices, on_device(): lax.all_gather(shared_gate_weight, 'col', axis=0, tiled=True)  38 us
    all_to_all x1, waiting for transfers between devices, on_device(): lax.all_to_all(summed, 'col', split_axis=0, concat_axis=0, tiled=True)  27.9 us
    dot_general x1, matrix products, on_device(): jnp.einsum('sexf,efd->sexd', hidden, routed_down_weight, preferred_elemen...  15.4 us
    ppermute x4, waiting for transfers between devices, on_device(): lower.append(lax.ppermute(lower[-1] if lower else tokens, 'row', pairs))  12 us
    gather x1, local copies, waits for them, and re-layouts, on_device(): jnp.take(all_features, jnp.minimum(slot_token, token_count - 1), axis=0)  11 us
  transfers between devices with their start and end apart: 15, of which 9 were waited for; matrix products, arithmetic and copies ran while one was open for 16% of the time, Pallas kernels for 0%

profile of v1, /device:TPU:0, one launch (start us, length us, event | category | flops | bytes accessed | tf_op | source)
XLA Modules:
  0.0 461.4 jit_solution(3280560956052822374)
XLA Ops:
  6.5 0.8 compare_and_fusion.2
  8.0 1.6 gather_fusion.3
  9.6 0.7 broadcast_select_fusion
  11.2 3.6 collective-permute-start.4
  14.8 0.7 fusion.28
  17.7 5.5 %collective-permute-done.1 = bf16[256,256]{1,0:T(8,128)(2,1)S(1)} collective-permute-done((bf16[256,256]{1,0:T(8,128)(2,1)S(1)}, bf16[256,256]{1,0:T(8,128)(2,1)S(1)}, u32[]{:S(2)}, u32[]{:S(2)}) %collective-permute-start.1) | collective-permute-done | bytes 131104 | tf_op jit(solution)/shard_map/ppermute | solution.py:38
  23.3 3.0 collective-permute-start.5
  26.2 3.1 collective-permute-done.2
  29.3 3.0 collective-permute-start.6
  32.3 3.2 collective-permute-done.3
  35.7 1.6 gather_fusion
  37.2 1.3 copy.63
  38.6 11.0 %gather_fusion.1 = bf16[2048,2048]{1,0:T(8,128)(2,1)} fusion(bf16[256,2048]{1,0:T(8,128)(2,1)S(1)} %bitcast.105, s32[2048]{0:T(1024)S(1)} %broadcast_clamp_fusion), kind=kCustom, calls=%fused_computation.1 | custom fusion | bytes 16785408 | tf_op jit(solution)/shard_map/jit(_take)/gather | solution.py:114
  49.6 7.5 %select_select_fusion = bf16[16,2,64,2048]{3,2,1,0:T(8,128)(2,1)} fusion(bf16[16,2,64,2048]{3,2,1,0:T(8,128)(2,1)} %bitcast.111, pred[16,2,64]{2,1,0:T(4,128)(4,1)S(1)} %get-tuple-element.9, pred[16,2,64]{2,1,0:T(4,128)(4,1)S(1)} %get-tuple-element.10), kind=kLoop, calls=%fused_computation.5 | loop fusion | flops 8388608 | bytes 16781312 | tf_op jit(solution)/shard_map/jit(_where)/select_n | solution.py:115
  57.1 6.9 %all-to-all-start = ((bf16[16,2,64,2048]{3,2,1,0:T(8,128)(2,1)}), bf16[16,2,64,2048]{3,2,1,0:T(8,128)(2,1)}, u32[]{:S(2)}, u32[]{:S(2)}) async-start(bf16[16,2,64,2048]{3,2,1,0:T(8,128)(2,1)} %select_select_fusion), calls=%async_computation | async-start | bytes 16777216 | tf_op jit(solution)/shard_map/all_to_all | solution.py:117
  64.7 126.1 %all-to-all-done = bf16[16,2,64,2048]{3,2,1,0:T(8,128)(2,1)} async-done(((bf16[16,2,64,2048]{3,2,1,0:T(8,128)(2,1)}), bf16[16,2,64,2048]{3,2,1,0:T(8,128)(2,1)}, u32[]{:S(2)}, u32[]{:S(2)}) %all-to-all-start) | async-done | bytes 8388640 | tf_op jit(solution)/shard_map/all_to_all | solution.py:117
  190.7 7.4 %fusion.2 = f32[2,16,64,176]{3,2,1,0:T(8,128)} fusion(bf16[16,2,64,2048]{3,2,1,0:T(8,128)(2,1)} %all-to-all-done, bf16[2,2048,176]{1,2,0:T(8,128)(2,1)} %param.21), kind=kOutput, calls=%fused_computation.8 | convolution fusion | flops 1476395008 | bytes 11272192 | tf_op jit(solution)/shard_map/sexd,edf->sexf/dot_general | solution.py:118
  198.1 15.4 %convolution_bitcast_fusion = f32[16,2,64,2048]{3,2,0,1:T(8,128)} fusion(f32[2,16,64,176]{3,2,1,0:T(8,128)} %fusion.2, bf16[16,2,64,2048]{3,2,1,0:T(8,128)(2,1)} %all-to-all-done, bf16[2,176,2048]{2,1,0:T(8,128)(2,1)} %param.23, bf16[2,2048,176]{1,2,0:T(8,128)(2,1)} %param.22), kind=kOutput, calls=%fused_computation.10 | convolution fusion | flops 2954952704 | bytes 29491200 | tf_op jit(solution)/shard_map/sexf,efd->sexd/dot_general | solution.py:125
  215.8 1.7 fusion.19
  217.5 3.6 fusion.37
  221.1 38.0 %all-gather.5.cloned.1.call-done = bf16[2048,704]{0,1:T(8,128)(2,1)} async-done(((bf16[128,704]{0,1:T(8,128)(2,1)}), bf16[2048,704]{0,1:T(8,128)(2,1)}) %all-gather.5.cloned.1.call-update) | async-done | bytes 2883600 | tf_op jit(solution)/shard_map/all_gather | solution.py:92
  259.1 3.6 fusion.36
  262.7 48.2 %all-gather.11.cloned.1.call-done = bf16[704,2048]{1,0:T(8,128)(2,1)} async-done(((bf16[704,128]{1,0:T(8,128)(2,1)}), bf16[704,2048]{1,0:T(8,128)(2,1)}) %all-gather.11.cloned.1.call-update) | async-done | bytes 2883600 | tf_op jit(solution)/shard_map/all_gather | solution.py:105
  311.0 4.9 %convolution_multiply_fusion = f32[256,2048]{1,0:T(8,128)} fusion(bf16[704,2048]{1,0:T(8,128)(2,1)} %all-gather.11.cloned.1.call-done, f32[256,704]{0,1:T(8,128)} %fusion.37, bf16[256,256]{1,0:T(8,128)(2,1)S(1)} %fusion.19, bf16[256,704]{1,0:T(8,128)(2,1)S(1)} %bitcast_select_fusion, f32[256]{0:T(256)S(1)} %add_divide_fusion, f32[256,704]{0,1:T(8,128)} %fusion.36), kind=kOutput, calls=%fused_computation.11 | convolution fusion | flops 832438272 | bytes 6915072 | tf_op jit(solution)/shard_map/dot_general | solution.py:103
  315.9 88.8 %reduce-scatter.3.cloned.1.call-done = f32[16,2,64,256]{3,2,0,1:T(8,128)} async-done(((f32[16,2,64,2048]{3,2,0,1:T(8,128)}), f32[16,2,64,256]{3,2,0,1:T(8,128)}) %reduce-scatter.3.cloned.1.call-update) | async-done | bytes 2097168 | tf_op jit(solution)/shard_map/reduce_scatter | solution.py:129
  404.7 3.2 copy.56
  407.9 7.0 %all-to-all-start.1 = ((f32[16,2,64,256]{3,2,1,0:T(8,128)}), f32[16,2,64,256]{3,2,1,0:T(8,128)}, u32[]{:S(2)}, u32[]{:S(2)}) async-start(f32[16,2,64,256]{3,2,1,0:T(8,128)} %copy.56), calls=%async_computation.2 | async-start | bytes 4194304 | tf_op jit(solution)/shard_map/all_to_all | solution.py:132
  416.1 27.9 %all-to-all-done.1 = f32[16,2,64,256]{3,2,1,0:T(8,128)} async-done(((f32[16,2,64,256]{3,2,1,0:T(8,128)}), f32[16,2,64,256]{3,2,1,0:T(8,128)}, u32[]{:S(2)}, u32[]{:S(2)}) %all-to-all-start.1) | async-done | bytes 2097184 | tf_op jit(solution)/shard_map/all_to_all | solution.py:132
  444.0 5.1 %gather_fusion.2 = f32[1024,256]{1,0:T(8,128)S(1)} fusion(f32[2048,256]{1,0:T(8,128)} %bitcast.24, s32[1024]{0:T(1024)S(1)} %broadcast_clamp_fusion.1), kind=kCustom, calls=%fused_computation.2 | custom fusion | bytes 2101248 | tf_op jit(solution)/shard_map/jit(_take)/gather | solution.py:134
  449.0 1.3 reshape.225
  450.3 2.5 multiply_reduce_fusion
  452.9 1.7 add.103
  (88 shorter events, 7.8 us)
Async XLA Ops:
  6.5 207.9 %copy-start = (bf16[64,16,704]{2,1,0:T(8,128)(2,1)S(1)}, bf16[64,16,704]{2,1,0:T(8,128)(2,1)}, u32[]{:S(2)}) copy-start(bf16[64,16,704]{2,1,0:T(8,128)(2,1)} %param.25) | copy-start | bytes 4325380
  6.5 29.0 %copy-start.2 = (bf16[256,256]{1,0:T(8,128)(2,1)S(1)}, bf16[256,256]{1,0:T(8,128)(2,1)}, u32[]{:S(2)}) copy-start(bf16[256,256]{1,0:T(8,128)(2,1)} %param.15) | copy-start | bytes 393220
  6.5 209.2 %all-gather.9.cloned.1.call-start = ((), (), s32[]{:S(2)}) async-start(), calls=%async_computation.7 | async-start | bytes 1179648 | tf_op jit(solution)/shard_map/all_gather | solution.py:77
  10.4 207.1 %all-gather.7.cloned.1.call-start = ((), (), s32[]{:S(2)}) async-start(), calls=%async_computation.6 | async-start | bytes 3063808 | tf_op jit(solution)/shard_map/all_gather | solution.py:97
  11.1 248.0 %all-gather.5.cloned.1.call-start = ((), (), s32[]{:S(2)}) async-start(), calls=%async_computation.5 | async-start | bytes 3063808 | tf_op jit(solution)/shard_map/all_gather | solution.py:92
  11.2 6.5 %collective-permute-start = (bf16[256,256]{1,0:T(8,128)(2,1)}, bf16[256,256]{1,0:T(8,128)(2,1)S(1)}, u32[]{:S(2)}, u32[]{:S(2)}) collective-permute-start(bf16[256,256]{1,0:T(8,128)(2,1)} %param.15), channel_id=1, source_target_pairs={{0,16},{16,32},{32,48},{48,64},{64,80},{80,96},{96,112},{112,0},{1... | collective-permute-start | bytes 393224 | tf_op jit(solution)/shard_map/ppermute | solution.py:38
  11.2 12.1 %collective-permute-start.4 = (bf16[256,256]{1,0:T(8,128)(2,1)}, bf16[256,256]{1,0:T(8,128)(2,1)S(1)}, u32[]{:S(2)}, u32[]{:S(2)}) collective-permute-start(bf16[256,256]{1,0:T(8,128)(2,1)} %param.15), channel_id=1, source_target_pairs={{16,0},{32,16},{48,32},{64,48},{80,64},{96,80},{112,96},{0,112},{1... | collective-permute-start | bytes 393224 | tf_op jit(solution)/shard_map/ppermute | solution.py:40
  17.6 5.6 %collective-permute-start.1 = (bf16[256,256]{1,0:T(8,128)(2,1)S(1)}, bf16[256,256]{1,0:T(8,128)(2,1)S(1)}, u32[]{:S(2)}, u32[]{:S(2)}) collective-permute-start(bf16[256,256]{1,0:T(8,128)(2,1)S(1)} %collective-permute-done), channel_id=1, source_target_pairs={{0,16},{16,32},{32,48},{48,64},{64,80},{80,96},{96,112},{112,0},{1... | collective-permute-start | bytes 393224 | tf_op jit(solution)/shard_map/ppermute | solution.py:38
  23.2 6.0 %collective-permute-start.2 = (bf16[256,256]{1,0:T(8,128)(2,1)S(1)}, bf16[256,256]{1,0:T(8,128)(2,1)S(1)}, u32[]{:S(2)}, u32[]{:S(2)}) collective-permute-start(bf16[256,256]{1,0:T(8,128)(2,1)S(1)} %collective-permute-done.1), channel_id=1, source_target_pairs={{0,16},{16,32},{32,48},{48,64},{64,80},{80,96},{96,112},{112,0},{1... | collective-permute-start | bytes 393224 | tf_op jit(solution)/shard_map/ppermute | solution.py:38
  23.3 6.1 %collective-permute-start.5 = (bf16[256,256]{1,0:T(8,128)(2,1)S(1)}, bf16[256,256]{1,0:T(8,128)(2,1)S(1)}, u32[]{:S(2)}, u32[]{:S(2)}) collective-permute-start(bf16[256,256]{1,0:T(8,128)(2,1)S(1)} %collective-permute-done.4), channel_id=1, source_target_pairs={{16,0},{32,16},{48,32},{64,48},{80,64},{96,80},{112,96},{0,112},{1... | collective-permute-start | bytes 393224 | tf_op jit(solution)/shard_map/ppermute | solution.py:40
  29.3 6.2 %collective-permute-start.3 = (bf16[256,256]{1,0:T(8,128)(2,1)S(1)}, bf16[256,256]{1,0:T(8,128)(2,1)S(1)}, u32[]{:S(2)}, u32[]{:S(2)}) collective-permute-start(bf16[256,256]{1,0:T(8,128)(2,1)S(1)} %collective-permute-done.2), channel_id=1, source_target_pairs={{0,16},{16,32},{32,48},{48,64},{64,80},{80,96},{96,112},{112,0},{1... | collective-permute-start | bytes 393224 | tf_op jit(solution)/shard_map/ppermute | solution.py:38
  29.3 6.3 %collective-permute-start.6 = (bf16[256,256]{1,0:T(8,128)(2,1)S(1)}, bf16[256,256]{1,0:T(8,128)(2,1)S(1)}, u32[]{:S(2)}, u32[]{:S(2)}) collective-permute-start(bf16[256,256]{1,0:T(8,128)(2,1)S(1)} %collective-permute-done.5), channel_id=1, source_target_pairs={{16,0},{32,16},{48,32},{64,48},{80,64},{96,80},{112,96},{0,112},{1... | collective-permute-start | bytes 393224 | tf_op jit(solution)/shard_map/ppermute | solution.py:40
  57.1 133.6 %all-to-all-start = ((bf16[16,2,64,2048]{3,2,1,0:T(8,128)(2,1)}), bf16[16,2,64,2048]{3,2,1,0:T(8,128)(2,1)}, u32[]{:S(2)}, u32[]{:S(2)}) async-start(bf16[16,2,64,2048]{3,2,1,0:T(8,128)(2,1)} %select_select_fusion), calls=%async_computation | async-start | bytes 16777216 | tf_op jit(solution)/shard_map/all_to_all | solution.py:117
  64.0 246.9 %all-gather.11.cloned.1.call-start = ((), (), s32[]{:S(2)}) async-start(), calls=%async_computation.8 | async-start | bytes 3063808 | tf_op jit(solution)/shard_map/all_gather | solution.py:105
  64.6 340.1 %reduce-scatter.3.cloned.1.call-start = ((), (), s32[]{:S(2)}) async-start(), calls=%async_computation.4 | async-start | bytes 18874368 | tf_op jit(solution)/shard_map/reduce_scatter | solution.py:129
  213.5 0.7 copy-start.4
  213.5 0.7 copy-start.5
  213.5 1.6 copy-start.6
  213.6 239.3 %reduce-scatter.5.cloned.1.call-start = ((), (), s32[]{:S(2)}) async-start(), calls=%async_computation.9 | async-start | bytes 2359296 | tf_op jit(solution)/shard_map/reduce_scatter | solution.py:130
  407.9 7.1 %copy-start.3 = (s32[256,4]{0,1:T(4,128)S(1)}, s32[256,4]{0,1:T(4,128)}, u32[]{:S(2)}) copy-start(s32[256,4]{0,1:T(4,128)} %param.26) | copy-start | bytes 12292
  407.9 7.6 %copy-start.1 = (bf16[2048,32]{0,1:T(8,128)(2,1)S(1)}, bf16[2048,32]{0,1:T(8,128)(2,1)}, u32[]{:S(2)}) copy-start(bf16[2048,32]{0,1:T(8,128)(2,1)} %param.16) | copy-start | bytes 393220
  407.9 36.1 %all-to-all-start.1 = ((f32[16,2,64,256]{3,2,1,0:T(8,128)}), f32[16,2,64,256]{3,2,1,0:T(8,128)}, u32[]{:S(2)}, u32[]{:S(2)}) async-start(f32[16,2,64,256]{3,2,1,0:T(8,128)} %copy.56), calls=%async_computation.2 | async-start | bytes 4194304 | tf_op jit(solution)/shard_map/all_to_all | solution.py:132
Sparse Core Ops, SparseCore 0:
  10.5 27.2 all-gather.8
  39.9 140.6 all-gather.6
  182.7 76.3 all-gather.4
  261.1 49.8 all-gather.10
  313.3 91.3 reduce-scatter.2
  407.0 34.4 reduce-scatter.4
